TPU v7x, 128 devices: a whole 4x4x4 slice. The times are simulated.
128 devices in a mesh: req: 16 (over z, x), head: 8 (over y, core).
Axes of the slice: x: 4, y: 4, z: 4, core: 2. Of those that a mesh axis runs over, the one named last changes fastest.
Arguments:
- tokens: bfloat16 [256, 1280], P('req'), may hold values from -6 to 6
- w_qkv: bfloat16 [2, 3, 1280, 1280], P(None, None, 'head'), may hold values from -0.15625 to 0.15625
- w_out: bfloat16 [2, 1280, 1280], P(None, 'head'), may hold values from -0.15625 to 0.15625
- w_up: bfloat16 [2, 1280, 1280], P(None, 'head'), may hold values from -0.15625 to 0.15625
- w_down: bfloat16 [2, 1280, 1280], P(None, 'head'), may hold values from -0.15625 to 0.15625
- gain_attn: float32 [2, 1280], replicated, may hold values from 0.1 to 1.9
- gain_mlp: float32 [2, 1280], replicated, may hold values from 0.1 to 1.9
- suffix_cache: bfloat16 [2, 2, 512, 1280, 128], P(None, None, 'req', 'head'), may hold values from -110 to 110
- prompt_cache: bfloat16 [2, 2, 96, 1280, 128], P(None, None, 'req', 'head'), may hold values from -110 to 110
- suffix_table: int32 [16, 32], P('req'), may hold values from 0 to 31, each once within a row
- prompt_owner: int32 [96], replicated, may hold values from 0 to 95, each once
- suffix_len: int32 [256], P('req'), may hold values from 1 to 256, 32768 in all
- group_id: int32 [256], P('req'), may hold values from 0 to 23, never falling along the last dimension, each value on 1 to 16 neighbouring positions
Outputs:
- hidden: bfloat16 [256, 1280], P('req')
- new_cache: bfloat16 [2, 2, 256, 1280], P(None, None, 'req', 'head')
Inputs may be any that keep to these rules, and one draw needn't show every extreme that they name: `suffix_table`: each row holds every number once. `prompt_owner`: each number once. `group_id`: never falls from one request to the next; every group has 1 to 16 requests, one group exactly 16.
All inputs are finite; a program needn't handle non-finite values. No bound on the sum of `suffix_len` on one device may be relied on, other than what follows from the above.
Results may differ from a plain program's by a relative error of at most 0.019.
The roundings to bfloat16 on the way count: a program that leaves them out, or rounds other values in their place, can miss the bound.
Values may be sent and summed in bfloat16 or wider, within the bound.
No kernel may reach another device: no remote copies, remote signals or barrier semaphores. Data moves between devices by JAX's collectives and lax.ppermute only.
A program may use at most 128 MiB of HBM per device.

v0:
```python
import math
import jax
import jax.numpy as jnp
from jax import lax
from jax.sharding import PartitionSpec as P

HD = 80
PPAGES = 4
NEG_FLOOR = -1e30


def root_norm(values, gains):
    factor = lax.rsqrt(jnp.mean(values * values, axis=-1, keepdims=True) + 1e-06)
    return values * factor * gains


def page_groups(prompt_owner, count, page_len):
    owners = prompt_owner // PPAGES
    return jnp.repeat(owners, page_len, total_repeat_length=count * page_len)


def attend(
    query, key_new, val_new, layer_suffix, layer_prompt, pages, valid, group_id, prompt_owner
):
    row_count = query.shape[0]
    head_count = query.shape[1] // HD
    scale = 1.0 / math.sqrt(HD)
    page_len = layer_suffix.shape[3]
    own_pages = pages.shape[1]
    query_heads = query.reshape(row_count, head_count, HD)
    key_heads = key_new.reshape(row_count, head_count, HD)
    val_heads = val_new.reshape(row_count, head_count, HD)
    gathered_pages = layer_suffix[:, pages].reshape(
        2, row_count, own_pages, head_count, HD, page_len
    )
    scores = (
        jnp.einsum(
            "rhd,rphdt->rhpt", query_heads, gathered_pages[0], preferred_element_type=jnp.float32
        ).reshape(row_count, head_count, own_pages * page_len)
        * scale
    )
    own = (
        jnp.einsum("rhd,rhd->rh", query_heads, key_heads, preferred_element_type=jnp.float32)
        * scale
    )
    mask = valid[:, None, :]
    local_top = jnp.maximum(jnp.max(jnp.where(mask, scores, NEG_FLOOR), axis=-1), own)
    weights = jnp.exp(jnp.where(mask, scores - local_top[..., None], NEG_FLOOR))
    own_weight = jnp.exp(own - local_top)
    total = jnp.sum(weights, axis=-1) + own_weight
    weight_pages = weights.astype(jnp.bfloat16).reshape(row_count, head_count, own_pages, page_len)
    mixed = jnp.einsum(
        "rhpt,rphdt->rhd", weight_pages, gathered_pages[1], preferred_element_type=jnp.float32
    )
    mixed = mixed + jnp.einsum(
        "rh,rhd->rhd",
        own_weight.astype(jnp.bfloat16),
        val_heads,
        preferred_element_type=jnp.float32,
    )
    piece = lax.all_gather(layer_prompt, "req", axis=1, tiled=True)
    count = piece.shape[1]
    key_group = page_groups(prompt_owner, count, page_len)
    keys = piece[0].reshape(count, head_count, HD, page_len)
    vals = piece[1].reshape(count, head_count, HD, page_len)
    block = (
        jnp.einsum("rhd,phdt->rhpt", query_heads, keys, preferred_element_type=jnp.float32).reshape(
            row_count, head_count, count * page_len
        )
        * scale
    )
    match = (group_id[:, None] == key_group[None, :])[:, None, :]
    new_top = jnp.maximum(local_top, jnp.max(jnp.where(match, block, NEG_FLOOR), axis=-1))
    block_weights = jnp.exp(jnp.where(match, block - new_top[..., None], NEG_FLOOR))
    factor = jnp.exp(local_top - new_top)
    new_total = total * factor + jnp.sum(block_weights, axis=-1)
    block_rounded = block_weights.astype(jnp.bfloat16).reshape(
        row_count, head_count, count, page_len
    )
    new_mixed = mixed * factor[..., None] + jnp.einsum(
        "rhpt,phdt->rhd", block_rounded, vals, preferred_element_type=jnp.float32
    )
    return (new_mixed / new_total[..., None]).reshape(row_count, -1).astype(jnp.bfloat16)


def add_branch(residual, partial_value, gains, closing):
    residual = residual + lax.psum(partial_value, "head")
    if closing:
        normed = None
    else:
        normed = root_norm(residual, gains).astype(jnp.bfloat16)
    return (residual, normed)


def local(
    tokens,
    w_qkv,
    w_out,
    w_up,
    w_down,
    gain_attn,
    gain_mlp,
    suffix_cache,
    prompt_cache,
    suffix_table,
    prompt_owner,
    suffix_len,
    group_id,
):
    row_count = tokens.shape[0]
    layer_count = w_qkv.shape[0]
    width_here = w_qkv.shape[2]
    model_width = w_qkv.shape[3]
    pages = suffix_table[0].reshape(row_count, -1)
    span = pages.shape[1] * suffix_cache.shape[4]
    valid = jnp.arange(span, dtype=jnp.int32)[None, :] < suffix_len[:, None]
    whole = tokens.astype(jnp.float32)
    normed = root_norm(whole, gain_attn[0]).astype(jnp.bfloat16)
    residual = whole
    new_keys = []
    new_vals = []
    for layer in range(layer_count):
        projected = jnp.einsum(
            "rd,kd->rk",
            normed,
            w_qkv[layer].reshape(3 * width_here, model_width),
            preferred_element_type=jnp.float32,
        )
        projected = projected.reshape(row_count, 3, width_here).astype(jnp.bfloat16)
        query = projected[:, 0]
        key_new = projected[:, 1]
        val_new = projected[:, 2]
        new_keys.append(key_new)
        new_vals.append(val_new)
        attended = attend(
            query,
            key_new,
            val_new,
            suffix_cache[layer],
            prompt_cache[layer],
            pages,
            valid,
            group_id,
            prompt_owner,
        )
        partial_value = jnp.dot(attended, w_out[layer], preferred_element_type=jnp.float32)
        residual, normed = add_branch(residual, partial_value, gain_mlp[layer], False)
        hidden_units = jax.nn.silu(
            jnp.einsum("rd,fd->rf", normed, w_up[layer], preferred_element_type=jnp.float32)
        ).astype(jnp.bfloat16)
        partial_value = jnp.dot(hidden_units, w_down[layer], preferred_element_type=jnp.float32)
        closing = layer == layer_count - 1
        next_gains = gain_attn[layer] if closing else gain_attn[layer + 1]
        residual, normed = add_branch(residual, partial_value, next_gains, closing)
    hidden = residual.astype(jnp.bfloat16)
    new_cache = jnp.stack([jnp.stack(new_keys), jnp.stack(new_vals)], axis=1)
    return (hidden, new_cache)


def solution(mesh):
    placed = (
        P("req", None),
        P(None, None, "head", None),
        P(None, "head", None),
        P(None, "head", None),
        P(None, "head", None),
        P(),
        P(),
        P(None, None, "req", "head", None),
        P(None, None, "req", "head", None),
        P("req", None),
        P(),
        P("req"),
        P("req"),
    )
    return jax.shard_map(
        local,
        mesh=mesh,
        in_specs=placed,
        out_specs=(P("req", None), P(None, None, "req", "head")),
        check_vma=False,
    )
```

profile of v0, /device:TPU:1, one launch (start us, length us, event | category | flops | bytes accessed | tf_op | source)
XLA Modules:
  0.0 431.9 jit_solution(11187171101283764259)
XLA Ops:
  7.3 2.4 fusion.147
  9.7 0.0 all-reduce.5.cloned.1.call-start
  9.8 0.1 fusion.94
  9.9 0.5 fusion.38
  10.4 0.1 reshape_squeeze.31
  10.5 0.1 reshape.287
  10.6 0.1 reshape_squeeze.33
  10.7 0.1 fusion.125
  10.8 0.1 copy.53
  10.8 0.5 broadcast.282
  11.4 0.7 reduce.26
  12.0 0.1 reshape_squeeze.32
  12.1 0.1 reshape.237
  12.2 0.1 reshape.225
  12.3 73.0 %gather_fusion.2 = s32[12288]{0:T(1024)S(1)} fusion(s32[96]{0:T(128)S(1)} %and_select_fusion, s32[12288]{0:T(1024)S(1)} %fusion.97), kind=kCustom, calls=%fused_computation.clone | custom fusion | bytes 147456 | tf_op jit(solution)/shard_map/jit(_take)/gather | solution.py:19
  85.4 4.6 %slice_bitcast_fusion = (bf16[2,32,160,128]{3,2,1,0:T(8,128)(2,1)S(1)}, bf16[2,32,160,128]{3,2,1,0:T(8,128)(2,1)}) fusion(bf16[2,2,32,160,128]{4,3,2,1,0:T(8,128)(2,1)} %param.26), kind=kLoop, calls=%fused_computation.11 | loop fusion | bytes 10485760 | tf_op jit(solution)/shard_map/squeeze | solution.py:139
  90.0 4.1 gather_fusion
  94.2 0.1 broadcast_compare_fusion.1
  94.2 1.9 fusion.146
  96.1 0.3 fusion.26
  96.4 0.1 select_reduce_fusion.1
  96.5 0.2 fusion.116
  96.7 0.2 broadcast_compare_fusion
  96.9 0.4 fusion.24
  97.3 3.6 fusion.144
  101.0 0.8 fusion.11
  101.7 0.5 fusion.28
  102.3 1.2 fusion.62
  103.5 0.1 convert_element_type.71
  103.6 1.8 fusion.86
  105.5 0.7 all-gather.7.cloned.1.call-update
  106.3 2.4 gather_fusion.1
  108.8 3.0 fusion.145
  111.8 53.2 %all-reduce.5.cloned.1.call-done = f32[16,1280]{1,0:T(8,128)} async-done(((f32[16,1280]{1,0:T(8,128)}), f32[16,1280]{1,0:T(8,128)}) %all-reduce.5.cloned.1.call-update) | async-done | bytes 81936 | tf_op jit(solution)/shard_map/psum | solution.py:87
  165.0 1.0 multiply_reduce_fusion.2
  166.1 2.2 fusion.82
  168.3 0.0 all-reduce.9.cloned.1.call-start
  168.3 67.2 %all-gather.7.cloned.1.call-done = bf16[1,2,96,160,128]{4,3,2,1,0:T(8,128)(2,1)} async-done(((bf16[1,2,6,160,128]{4,3,2,1,0:T(8,128)(2,1)}), bf16[1,2,96,160,128]{4,3,2,1,0:T(8,128)(2,1)}) %all-gather.7.cloned.1.call-update) | async-done | bytes 7864336 | tf_op jit(solution)/shard_map/all_gather | solution.py:61
  235.5 5.4 %fusion.143 = (bf16[1,1,96,160,128]{4,3,2,1,0:T(8,128)(2,1)}, bf16[1,1,96,160,128]{4,3,2,1,0:T(8,128)(2,1)}) fusion(bf16[1,2,96,160,128]{4,3,2,1,0:T(8,128)(2,1)} %all-gather.7.cloned.1.call-done), kind=kLoop, calls=%fused_computation.177 | loop fusion | bytes 15728640 | tf_op jit(solution)/shard_map/slice | solution.py:64
  241.0 52.7 %all-reduce.7.cloned.1.call-done = f32[16,1280]{1,0:T(8,128)} async-done(((f32[16,1280]{1,0:T(8,128)}), f32[16,1280]{1,0:T(8,128)}) %all-reduce.7.cloned.1.call-update) | async-done | bytes 81936 | tf_op jit(solution)/shard_map/psum | solution.py:87
  293.7 1.0 multiply_reduce_fusion.1
  294.7 1.7 fusion.41
  296.4 0.1 reshape_squeeze.36
  296.6 0.1 reshape.289
  296.6 0.1 reshape_squeeze.37
  296.7 0.1 fusion.123
  296.8 0.1 copy.66
  296.9 0.3 fusion.22
  297.2 0.1 select_reduce_fusion
  297.3 0.2 fusion.118
  297.5 2.9 fusion.8
  300.3 0.1 reshape.226
  300.4 1.7 fusion.20
  302.2 0.6 fusion.30
  302.7 3.3 fusion.65
  306.1 0.1 convert_element_type.80
  306.2 1.8 fusion.80
  308.0 0.0 all-reduce.11.cloned.1.call-start
  308.1 56.1 %all-reduce.9.cloned.1.call-done = f32[16,1280]{1,0:T(8,128)} async-done(((f32[16,1280]{1,0:T(8,128)}), f32[16,1280]{1,0:T(8,128)}) %all-reduce.9.cloned.1.call-update) | async-done | bytes 81936 | tf_op jit(solution)/shard_map/psum | solution.py:87
  364.2 1.0 multiply_reduce_fusion
  365.2 2.2 fusion.76
  367.4 0.6 copy.45
  368.0 55.5 %all-reduce.11.cloned.1.call-done = f32[16,1280]{1,0:T(8,128)} async-done(((f32[16,1280]{1,0:T(8,128)}), f32[16,1280]{1,0:T(8,128)}) %all-reduce.11.cloned.1.call-update) | async-done | bytes 81936 | tf_op jit(solution)/shard_map/psum | solution.py:87
  423.5 1.5 add_convert_fusion
  (53 shorter events, 0.5 us)
Async XLA Ops:
  7.2 2.6 copy-start.4
  7.2 2.6 copy-start.2
  7.2 2.7 copy-start.3
  7.2 4.2 copy-start.8
  7.2 90.1 %all-gather.5.cloned.1.call-start = ((), (), s32[]{:S(2)}) async-start(), calls=%async_computation.4 | async-start | bytes 8355840 | tf_op jit(solution)/shard_map/all_gather | solution.py:61
  9.6 2.7 copy-start.9
  9.7 155.4 %all-reduce.5.cloned.1.call-start = ((), (), s32[]{:S(2)}) async-start(), calls=%async_computation | async-start | bytes 163840 | tf_op jit(solution)/shard_map/psum | solution.py:87
  90.0 4.2 copy-start.7
  94.2 2.5 copy-start.6
  105.5 130.1 %all-gather.7.cloned.1.call-start = ((), (), s32[]{:S(2)}) async-start(), calls=%async_computation.5 | async-start | bytes 8355840 | tf_op jit(solution)/shard_map/all_gather | solution.py:61
  106.2 187.5 %all-reduce.7.cloned.1.call-start = ((), (), s32[]{:S(2)}) async-start(), calls=%async_computation.1 | async-start | bytes 163840 | tf_op jit(solution)/shard_map/psum | solution.py:87
  106.2 2.5 copy-start.5
  108.7 57.3 %copy-start = (bf16[2,160,1280]{2,1,0:T(8,128)(2,1)S(1)}, bf16[2,160,1280]{2,1,0:T(8,128)(2,1)}, u32[]{:S(2)}) copy-start(bf16[2,160,1280]{2,1,0:T(8,128)(2,1)} %param.23) | copy-start | bytes 2457604
  168.3 125.4 %copy-start.1 = (f32[16,1280]{1,0:T(8,128)S(1)}, f32[16,1280]{1,0:T(8,128)}, u32[]{:S(2)}) copy-start(f32[16,1280]{1,0:T(8,128)} %all-reduce.5.cloned.1.call-done) | copy-start | bytes 245764
  168.3 195.9 %all-reduce.9.cloned.1.call-start = ((), (), s32[]{:S(2)}) async-start(), calls=%async_computation.2 | async-start | bytes 163840 | tf_op jit(solution)/shard_map/psum | solution.py:87
  308.0 115.5 %all-reduce.11.cloned.1.call-start = ((), (), s32[]{:S(2)}) async-start(), calls=%async_computation.3 | async-start | bytes 163840 | tf_op jit(solution)/shard_map/psum | solution.py:87
Sparse Core Ops, SparseCore 0:
  10.2 71.6 all-gather.4
  105.6 59.4 all-reduce.4
  167.2 68.3 all-gather.6
  237.7 55.9 all-reduce.6
  308.1 55.9 all-reduce.8
  367.5 55.9 all-reduce.10
where the time goes:
time: 433 us; the launch traced here: 432 us
  waiting for transfers between devices  286 us (66%)
  local copies, waits for them, and re-layouts  103 us (24%)
  matrix products  21.1 us (5%)
  between operations  14.4 us (3%)
  other arithmetic  7.59 us (2%)
    psum x4, waiting for transfers between devices, add_branch(): residual = residual + lax.psum(partial_value, 'head')  218 us
    gather x1, local copies, waits for them, and re-layouts, page_groups(): return jnp.repeat(owners, page_len, total_repeat_length=count * page_len)  73 us
    all_gather x2, waiting for transfers between devices, attend(): piece = lax.all_gather(layer_prompt, 'req', axis=1, tiled=True)  67.2 us
    slice x2, local copies, waits for them, and re-layouts, attend(): keys = piece[0].reshape(count, head_count, HD, page_len)  9.05 us
  transfers between devices with their start and end apart: 6, of which 5 were waited for; matrix products, arithmetic and copies ran while one was open for 24% of the time, Pallas kernels for 0%

commit v1 on v0

--- a/solution.py
+++ b/solution.py
@@ -84,7 +84,7 @@
 
 
 def add_branch(residual, partial_value, gains, closing):
-    residual = residual + lax.psum(partial_value, "head")
+    residual = residual + jnp.sum(lax.all_gather(partial_value, "head"), axis=0)
     if closing:
         normed = None
     else:

time: 433 us -> 200 us (0.46)
  waiting for transfers between devices: 286 us -> 7.74 us
  blocking collectives: 0 us -> 56.1 us
  matrix products: 21.1 us -> 14 us
    psum x4 -> x0, waiting for transfers between devices: 218 us -> none  [add_branch(): residual = residual + lax.psum(partial_value, 'head')]
    all_gather x2, waiting for transfers between devices: 67.2 us -> 7.02 us  [attend(): piece = lax.all_gather(layer_prompt, 'req', axis=1, tiled=True)]
    all_gather x0 -> x4, blocking collectives: none -> 56.1 us  [add_branch(): residual = residual + jnp.sum(lax.all_gather(partial_value, 'head'), axis=0)]
    slice x2, local copies, waits for them, and re-layouts: 4.94 us -> 0.6 us  [attend(): gathered_pages[1]]
  transfers between devices with their start and end apart: 6 -> 2, of which waited for: 5 -> 1; matrix products, arithmetic and copies ran while one was open for 24% -> 53% of each run, Pallas kernels for 0% -> 0%
where the time goes in v1:
time: 200 us; the launch traced here: 199 us
  local copies, waits for them, and re-layouts  99.7 us (50%)
  blocking collectives  56.1 us (28%)
  between operations  14.4 us (7%)
  matrix products  14 us (7%)
  waiting for transfers between devices  7.74 us (4%)
  other arithmetic  7.09 us (4%)
    gather x1, local copies, waits for them, and re-layouts, page_groups(): return jnp.repeat(owners, page_len, total_repeat_length=count * page_len)  73 us
    all_gather x4, blocking collectives, add_branch(): residual = residual + jnp.sum(lax.all_gather(partial_value, 'head'), axis=0)  56.1 us
    slice x2, local copies, waits for them, and re-layouts, attend(): keys = piece[0].reshape(count, head_count, HD, page_len)  8.51 us
    all_gather x2, waiting for transfers between devices, attend(): piece = lax.all_gather(layer_prompt, 'req', axis=1, tiled=True)  7.02 us
    gather x2, local copies, waits for them, and re-layouts, attend(): layer_suffix[:, pages]  6.43 us
    dot_general x2, matrix products, attend(): jnp.einsum('rhpt,phdt->rhd', block_rounded, vals, preferred_element_type=...  4.6 us
    squeeze x1, local copies, waits for them, and re-layouts, local(): suffix_cache[layer]  4.48 us
  transfers between devices with their start and end apart: 2, of which 1 were waited for; matrix products, arithmetic and copies ran while one was open for 53% of the time, Pallas kernels for 0%

profile of v1, /device:TPU:1, one launch (start us, length us, event | category | flops | bytes accessed | tf_op | source)
XLA Modules:
  0.0 199.2 jit_solution(14645486540904505171)
XLA Ops:
  7.2 2.3 %fusion.147 = (bf16[1,2,6,160,128]{4,3,2,1,0:T(8,128)(2,1)}, bf16[1,2,6,160,128]{4,3,2,1,0:T(8,128)(2,1)}) fusion(bf16[2,2,6,160,128]{4,3,2,1,0:T(8,128)(2,1)} %param.27), kind=kLoop, calls=%fused_computation.181 | loop fusion | bytes 1966080 | tf_op jit(solution)/shard_map/slice | solution.py:140
  9.7 0.7 all-gather.11.cloned.1.call-update
  10.4 0.6 slice_reduce_fusion.1
  11.0 0.1 fusion.94
  11.1 0.5 fusion.38
  11.6 0.6 slice_bitcast_fusion.5
  12.2 0.1 reshape_squeeze.31
  12.3 0.1 reshape.291
  12.4 0.1 reshape_squeeze.33
  12.5 0.1 fusion.125
  12.6 0.1 copy.53
  12.6 0.5 broadcast.282
  13.2 0.7 reduce.26
  13.8 0.1 reshape_squeeze.32
  13.9 0.1 reshape.237
  14.0 0.1 reshape.225
  14.1 4.5 %slice_bitcast_fusion = (bf16[2,32,160,128]{3,2,1,0:T(8,128)(2,1)S(1)}, bf16[2,32,160,128]{3,2,1,0:T(8,128)(2,1)}) fusion(bf16[2,2,32,160,128]{4,3,2,1,0:T(8,128)(2,1)} %param.26), kind=kLoop, calls=%fused_computation.11 | loop fusion | bytes 10485760 | tf_op jit(solution)/shard_map/squeeze | solution.py:139
  18.6 4.1 %gather_fusion = bf16[32,2,160,128]{3,2,1,0:T(8,128)(2,1)} fusion(bf16[2,32,160,128]{3,2,1,0:T(8,128)(2,1)} %get-tuple-element.50, s32[1024]{0:T(1024)S(1)} %pad_clamp_fusion), kind=kCustom, calls=%fused_computation.1 | custom fusion | bytes 5243008 | tf_op jit(solution)/shard_map/gather | solution.py:33
  22.7 2.3 %gather_fusion.1 = bf16[32,2,160,128]{3,2,1,0:T(8,128)(2,1)} fusion(bf16[2,32,160,128]{3,2,1,0:T(8,128)(2,1)S(1)} %get-tuple-element.49, s32[1024]{0:T(1024)S(1)} %pad_clamp_fusion), kind=kCustom, calls=%fused_computation.2 | custom fusion | bytes 5243008 | tf_op jit(solution)/shard_map/gather | solution.py:33
  25.1 73.0 %gather_fusion.2 = s32[12288]{0:T(1024)S(1)} fusion(s32[96]{0:T(128)S(1)} %and_select_fusion, s32[12288]{0:T(1024)S(1)} %fusion.97), kind=kCustom, calls=%fused_computation.clone | custom fusion | bytes 147456 | tf_op jit(solution)/shard_map/jit(_take)/gather | solution.py:19
  98.2 0.6 slice_reduce_fusion
  98.9 0.3 fusion.146
  99.2 0.3 fusion.26
  99.5 0.1 select_reduce_fusion.1
  99.6 0.2 fusion.116
  99.8 0.2 broadcast_compare_fusion
  100.0 0.4 fusion.24
  100.4 0.6 copy-done
  101.0 0.3 fusion.145
  101.3 3.7 %fusion.144 = (bf16[1,1,96,160,128]{4,3,2,1,0:T(8,128)(2,1)S(1)}, bf16[1,1,96,160,128]{4,3,2,1,0:T(8,128)(2,1)S(1)}) fusion(bf16[1,2,96,160,128]{4,3,2,1,0:T(8,128)(2,1)} %all-gather.9.cloned.1.call-done), kind=kLoop, calls=%fused_computation.178 | loop fusion | bytes 15728640 | tf_op jit(solution)/shard_map/slice | solution.py:64
  105.0 0.8 fusion.11
  105.8 0.5 fusion.28
  106.3 1.2 fusion.62
  107.6 0.1 convert_element_type.71
  107.7 1.2 fusion.86
  108.8 15.0 %all-gather.1 = f32[128,1280]{1,0:T(8,128)S(1)} all-gather(f32[16,1280]{1,0:T(8,128)S(1)} %fusion.86), channel_id=3, replica_groups=mesh['req'=16,'head'=8] {'head'}, dimensions={0}, use_global_device_ids=true | all-gather | bytes 737280 | tf_op jit(solution)/shard_map/all_gather | solution.py:87
  123.9 0.9 multiply_reduce_fusion.2
  124.8 2.3 %fusion.82 = f32[16,1280]{1,0:T(8,128)} fusion(bf16[2,160,1280]{2,1,0:T(8,128)(2,1)} %param.23, bf16[2,160,1280]{2,1,0:T(8,128)(2,1)} %param.22, f32[1280]{0:T(1024)} %get-tuple-element.30, f32[16]{0:T(128)S(1)} %add_rsqrt_fusion.2, f32[16,1280]{1,0:T(8,128)S(1)} %reduce_sum.111, bf16[16,1280]{1,0:T(8,128)(2,1)} %param.19), kind=kOutput, calls=%fused_computation.65 | convolution fusion | flops 13222400 | bytes 1032256 | tf_op jit(solution)/shard_map/dot_general | solution.py:151
  127.1 13.5 %all-gather.2 = f32[128,1280]{1,0:T(8,128)S(1)} all-gather(f32[16,1280]{1,0:T(8,128)} %fusion.82), channel_id=4, replica_groups=mesh['req'=16,'head'=8] {'head'}, dimensions={0}, use_global_device_ids=true | all-gather | bytes 737280 | tf_op jit(solution)/shard_map/all_gather | solution.py:87
  140.6 0.7 reduce_sum.113
  141.3 1.0 multiply_reduce_fusion.1
  142.3 1.8 fusion.41
  144.2 0.1 reshape_squeeze.36
  144.3 0.1 reshape.293
  144.4 0.1 reshape_squeeze.37
  144.4 0.1 fusion.123
  144.6 0.3 fusion.22
  144.9 0.1 select_reduce_fusion
  145.0 0.2 fusion.118
  145.2 7.0 %all-gather.11.cloned.1.call-done = bf16[1,2,96,160,128]{4,3,2,1,0:T(8,128)(2,1)} async-done(((bf16[1,2,6,160,128]{4,3,2,1,0:T(8,128)(2,1)}), bf16[1,2,96,160,128]{4,3,2,1,0:T(8,128)(2,1)}) %all-gather.11.cloned.1.call-update) | async-done | bytes 7864336 | tf_op jit(solution)/shard_map/all_gather | solution.py:61
  152.2 4.8 %fusion.143 = (bf16[1,1,96,160,128]{4,3,2,1,0:T(8,128)(2,1)S(1)}, bf16[1,1,96,160,128]{4,3,2,1,0:T(8,128)(2,1)}) fusion(bf16[1,2,96,160,128]{4,3,2,1,0:T(8,128)(2,1)} %all-gather.11.cloned.1.call-done), kind=kLoop, calls=%fused_computation.177 | loop fusion | bytes 15728640 | tf_op jit(solution)/shard_map/slice | solution.py:64
  157.0 0.8 fusion.8
  157.8 0.1 reshape.226
  157.9 0.4 fusion.20
  158.3 0.6 fusion.30
  158.9 3.4 %fusion.65 = bf16[16,2,80]{2,0,1:T(8,128)(2,1)S(1)} fusion(bf16[96,2,80,128]{3,2,1,0:T(8,128)(2,1)} %bitcast.212, f32[2,16,96,128]{3,1,2,0:T(8,128)S(1)} %get-tuple-element.74, f32[16,2]{0,1:T(2,128)S(1)} %max.15, pred[16,96,128]{2,0,1:T(8,128)(4,1)S(1)} %broadcast_compare_fusion, f32[16,2,1,80,1]{3,2,4,1,0:T(1,128)S(1)} %fusion.20, ...), kind=kOutput, calls=%fused_computation.52 | convolution fusion | flops 64109568 | bytes 5727744 | tf_op jit(solution)/shard_map/rhpt,phdt->rhd/dot_general | solution.py:80
  162.3 0.1 convert_element_type.80
  162.4 0.2 fusion.80
  162.6 14.4 %all-gather.4 = f32[128,1280]{1,0:T(8,128)S(1)} all-gather(f32[16,1280]{1,0:T(8,128)S(1)} %fusion.80), channel_id=6, replica_groups=mesh['req'=16,'head'=8] {'head'}, dimensions={0}, use_global_device_ids=true | all-gather | bytes 737280 | tf_op jit(solution)/shard_map/all_gather | solution.py:87
  177.1 0.1 multiply_reduce_fusion
  177.2 0.5 fusion.76
  177.7 13.2 %all-gather.5 = f32[128,1280]{1,0:T(8,128)S(1)} all-gather(f32[16,1280]{1,0:T(8,128)S(1)} %fusion.76), channel_id=7, replica_groups=mesh['req'=16,'head'=8] {'head'}, dimensions={0}, use_global_device_ids=true | all-gather | bytes 737280 | tf_op jit(solution)/shard_map/all_gather | solution.py:87
  191.0 0.6 add_convert_fusion
  191.7 0.6 copy.45
  (69 shorter events, 0.7 us)
Async XLA Ops:
  7.2 3.2 %copy-start.14 = (f32[2,1280]{1,0:T(2,128)S(1)}, f32[2,1280]{1,0:T(2,128)}, u32[]{:S(2)}) copy-start(f32[2,1280]{1,0:T(2,128)} %param.24) | copy-start | bytes 30724
  7.2 3.8 %copy-start.7 = (bf16[16,1280]{1,0:T(8,128)(2,1)S(1)}, bf16[16,1280]{1,0:T(8,128)(2,1)}, u32[]{:S(2)}) copy-start(bf16[16,1280]{1,0:T(8,128)(2,1)} %param.19) | copy-start | bytes 122884
  7.2 3.9 %copy-start.8 = (bf16[2,3,160,1280]{3,2,1,0:T(8,128)(2,1)S(1)}, bf16[2,3,160,1280]{3,2,1,0:T(8,128)(2,1)}, u32[]{:S(2)}) copy-start(bf16[2,3,160,1280]{3,2,1,0:T(8,128)(2,1)} %param.20) | copy-start | bytes 7372804
  7.2 94.1 %all-gather.9.cloned.1.call-start = ((), (), s32[]{:S(2)}) async-start(), calls=%async_computation | async-start | bytes 8355840 | tf_op jit(solution)/shard_map/all_gather | solution.py:61
  9.6 3.6 %copy-start.18 = (s32[1,32]{1,0:T(1,128)S(1)}, s32[1,32]{1,0:T(1,128)}, u32[]{:S(2)}) copy-start(s32[1,32]{1,0:T(1,128)} %param.28) | copy-start | bytes 388
  9.6 142.6 %all-gather.11.cloned.1.call-start = ((), (), s32[]{:S(2)}) async-start(), calls=%async_computation.1 | async-start | bytes 8355840 | tf_op jit(solution)/shard_map/all_gather | solution.py:61
  22.7 2.3 %copy-start.19 = (s32[96]{0:T(128)S(1)}, s32[96]{0:T(128)}, u32[]{:S(2)}) copy-start(s32[96]{0:T(128)} %param.29) | copy-start | bytes 1156
  25.1 73.1 %copy-start.15 = (f32[2,1280]{1,0:T(2,128)S(1)}, f32[2,1280]{1,0:T(2,128)}, u32[]{:S(2)}) copy-start(f32[2,1280]{1,0:T(2,128)} %param.25) | copy-start | bytes 30724
  25.1 73.7 %copy-start.17 = (s32[16]{0:T(128)S(1)}, s32[16]{0:T(128)}, u32[]{:S(2)}) copy-start(s32[16]{0:T(128)} %param.30) | copy-start | bytes 196
  25.1 73.8 %copy-start.1 = (bf16[32,2,160,128]{3,2,1,0:T(8,128)(2,1)S(1)}, bf16[32,2,160,128]{3,2,1,0:T(8,128)(2,1)}, u32[]{:S(2)}) copy-start(bf16[32,2,160,128]{3,2,1,0:T(8,128)(2,1)} %gather_fusion) | copy-start | bytes 7864324
  98.9 0.7 copy-start.9
  98.9 0.9 copy-start.16
  99.2 1.8 copy-start
  141.3 3.6 %copy-start.10 = (pred[16,2,128]{2,0,1:T(8,128)(4,1)S(1)}, pred[16,2,128]{2,0,1:T(8,128)(4,1)}, u32[]{:S(2)}) copy-start(pred[16,2,128]{2,0,1:T(8,128)(4,1)} %copy-done.9) | copy-start | bytes 12292
  142.3 14.7 %copy-start.5 = (f32[16,1280]{1,0:T(8,128)}, f32[16,1280]{1,0:T(8,128)S(1)}, u32[]{:S(2)}) copy-start(f32[16,1280]{1,0:T(8,128)S(1)} %get-tuple-element.40) | copy-start | bytes 245764
  158.9 3.5 %copy-start.4 = (bf16[2,160,1280]{2,1,0:T(8,128)(2,1)S(1)}, bf16[2,160,1280]{2,1,0:T(8,128)(2,1)}, u32[]{:S(2)}) copy-start(bf16[2,160,1280]{2,1,0:T(8,128)(2,1)} %param.21) | copy-start | bytes 2457604
  162.3 14.7 %copy-start.6 = (f32[16,1280]{1,0:T(8,128)S(1)}, f32[16,1280]{1,0:T(8,128)}, u32[]{:S(2)}) copy-start(f32[16,1280]{1,0:T(8,128)} %copy-done.5) | copy-start | bytes 245764
  162.3 14.9 %copy-start.2 = (bf16[2,160,1280]{2,1,0:T(8,128)(2,1)S(1)}, bf16[2,160,1280]{2,1,0:T(8,128)(2,1)}, u32[]{:S(2)}) copy-start(bf16[2,160,1280]{2,1,0:T(8,128)(2,1)} %param.23) | copy-start | bytes 2457604
  162.3 14.9 %copy-start.3 = (bf16[2,160,1280]{2,1,0:T(8,128)(2,1)S(1)}, bf16[2,160,1280]{2,1,0:T(8,128)(2,1)}, u32[]{:S(2)}) copy-start(bf16[2,160,1280]{2,1,0:T(8,128)(2,1)} %param.22) | copy-start | bytes 2457604
  162.3 14.9 %copy-start.11 = (f32[1280]{0:T(1024)S(1)}, f32[1280]{0:T(1024)}, u32[]{:S(2)}) copy-start(f32[1280]{0:T(1024)} %get-tuple-element.29) | copy-start | bytes 15364
  177.0 14.6 %copy-start.12 = (bf16[1,16,160]{2,1,0:T(8,128)(2,1)S(1)}, bf16[1,16,160]{2,1,0:T(8,128)(2,1)}, u32[]{:S(2)}) copy-start(bf16[1,16,160]{2,1,0:T(8,128)(2,1)} %get-tuple-element.61) | copy-start | bytes 15364
  177.1 14.6 %copy-start.13 = (bf16[1,16,160]{2,1,0:T(8,128)(2,1)S(1)}, bf16[1,16,160]{2,1,0:T(8,128)(2,1)}, u32[]{:S(2)}) copy-start(bf16[1,16,160]{2,1,0:T(8,128)(2,1)} %get-tuple-element.62) | copy-start | bytes 15364
Sparse Core Ops, SparseCore 0:
  10.1 71.6 all-gather.8
  84.0 68.1 all-gather.10
